TPU v7x, 512 devices: a whole 4x8x8 slice. The times are simulated.
512 devices in a mesh: seq: 32 (over x, y), row: 4 (over z_hi, core), col: 4 (over z_lo).
Axes of the slice: x: 4, y: 8, z: 8 (z_hi: 2, z_lo: 4; z = z_hi * 4 + z_lo), core: 2. Of those that a mesh axis runs over, the one named last changes fastest.
Arguments:
- queries: bfloat16 [2048, 8192], P(('seq', 'row', 'col')), may hold values from -6 to 6
- new_keys: bfloat16 [2048, 1024], P(('seq', 'row', 'col')), may hold values from -6 to 6
- new_values: bfloat16 [2048, 1024], P(('seq', 'row', 'col')), may hold values from -6 to 6
- positions: int32 [2048], P(('seq', 'row', 'col')), may hold values from 0 to 2047, each once
- cache_keys: bfloat16 [4096, 1024], P(('row', 'col')), may hold values from -6 to 6
- cache_values: bfloat16 [4096, 1024], P(('row', 'col')), may hold values from -6 to 6
- slab_start: int32 [1], replicated, may hold values from 2048 to 4096
Outputs:
- context: bfloat16 [2048, 8192], P(('seq', 'row', 'col'))
Inputs may be any that keep to these rules, and one draw needn't show every extreme that they name: positions holds every number of 0 to 2047 once.
All inputs are finite; a program needn't handle non-finite values.
Results may differ from a plain program's by a relative error of at most 0.0065.
Values may be sent and summed in bfloat16 or wider, within the bound.
No kernel may reach another device: no remote copies, remote signals or barrier semaphores. Data moves between devices by JAX's collectives and lax.ppermute only.
A program may use at most 64 MiB of HBM per device.

v0:
```python
import math
import jax
import jax.numpy as jnp
from jax import lax
from jax.sharding import PartitionSpec as P

HQ = 64
KVH = 8
HD = 128
far_position = 1073741824
masked_score = -1e30


def attend(carried, query_block, query_pos, key_rows, value_rows, key_pos, kv_dev):
    running_max, running_sum, running_out = carried
    key_count = key_rows.shape[0]
    head_size = query_block.shape[-1]
    score_scale = 1.0 / math.sqrt(head_size)
    block_size = 1024
    for offset in range(0, key_count, block_size):
        finish = min(key_count, offset + block_size)
        key_block = key_rows[offset:finish].reshape(finish - offset, kv_dev, head_size)
        value_block = value_rows[offset:finish].reshape(finish - offset, kv_dev, head_size)
        scores = (
            jnp.einsum("qghd,ngd->qghn", query_block, key_block, preferred_element_type=jnp.float32)
            * score_scale
        )
        allowed = (key_pos[offset:finish][None, :] <= query_pos[:, None])[:, None, None, :]
        updated = jnp.maximum(
            running_max, jnp.max(jnp.where(allowed, scores, masked_score), axis=-1)
        )
        exponent = jnp.where(allowed, jnp.exp(scores - updated[..., None]), 0.0)
        factor = jnp.exp(running_max - updated)
        running_sum = running_sum * factor + jnp.sum(exponent, axis=-1)
        running_out = running_out * factor[..., None] + jnp.einsum(
            "qghn,ngd->qghd",
            exponent.astype(jnp.bfloat16),
            value_block,
            preferred_element_type=jnp.float32,
        )
        running_max = updated
    return (running_max, running_sum, running_out)


def spread_heads(matrix, seq_count, kv_dev, head_size):
    row_count = matrix.shape[0]
    kv_heads = matrix.shape[1] // head_size
    repeat = max(1, seq_count * kv_dev // kv_heads)
    reshaped = matrix.reshape(row_count, kv_heads, head_size)
    reshaped = jnp.repeat(reshaped, repeat, axis=1)
    return reshaped


def on_device(queries, new_keys, new_values, positions, cache_keys, cache_values, slab_start):
    seq_count = lax.axis_size("seq")
    cell_count = lax.axis_size("row") * lax.axis_size("col")
    cell_index = lax.axis_index("row") * lax.axis_size("col") + lax.axis_index("col")
    heads_dev = HQ // seq_count
    group_size = HQ // KVH
    kv_dev = max(1, heads_dev // group_size)
    per_group = heads_dev // kv_dev
    tok_rows = queries.shape[0]
    first_pos = slab_start[0]
    kv_first = lax.axis_index("seq") * heads_dev // group_size
    every_pos = lax.all_gather(positions, ("seq", "row", "col"), axis=0, tiled=True)
    regrouped = lax.all_to_all(queries, "seq", split_axis=1, concat_axis=0, tiled=True)
    query_count = regrouped.shape[0]
    query_block = regrouped.reshape(query_count, kv_dev, per_group, HD)
    own_pos = (
        lax.dynamic_index_in_dim(
            every_pos.reshape(seq_count, cell_count, tok_rows), cell_index, 1, keepdims=False
        ).reshape(query_count)
        + first_pos
    )
    cache_key_head = lax.dynamic_slice_in_dim(cache_keys, kv_first * HD, kv_dev * HD, 1)
    cache_value_head = lax.dynamic_slice_in_dim(cache_values, kv_first * HD, kv_dev * HD, 1)
    carried = (
        jnp.full((query_count, kv_dev, per_group), masked_score, jnp.float32),
        jnp.zeros((query_count, kv_dev, per_group), jnp.float32),
        jnp.zeros((query_count, kv_dev, per_group, HD), jnp.float32),
    )
    grouped = (
        lax.all_gather(new_keys, ("row", "col"), axis=0, tiled=True),
        lax.all_gather(new_values, ("row", "col"), axis=0, tiled=True),
    )
    received = (
        lax.all_to_all(
            spread_heads(grouped[0], seq_count, kv_dev, HD),
            "seq",
            split_axis=1,
            concat_axis=0,
            tiled=True,
        ),
        lax.all_to_all(
            spread_heads(grouped[1], seq_count, kv_dev, HD),
            "seq",
            split_axis=1,
            concat_axis=0,
            tiled=True,
        ),
    )
    slab_keys = received[0].reshape(-1, kv_dev * HD)
    slab_values = received[1].reshape(-1, kv_dev * HD)
    carried = attend(
        carried, query_block, own_pos, slab_keys, slab_values, every_pos + first_pos, kv_dev
    )
    pieces = (
        lax.all_gather(cache_key_head, ("row", "col"), axis=0, tiled=True),
        lax.all_gather(cache_value_head, ("row", "col"), axis=0, tiled=True),
    )
    row_ids = jnp.arange(pieces[0].shape[0], dtype=jnp.int32)
    key_pos = jnp.where(row_ids < first_pos, row_ids, far_position)
    carried = attend(carried, query_block, own_pos, pieces[0], pieces[1], key_pos, kv_dev)
    running_max, running_sum, running_out = carried
    context = (
        (running_out / running_sum[..., None])
        .astype(jnp.bfloat16)
        .reshape(query_count, heads_dev * HD)
    )
    return lax.all_to_all(context, "seq", split_axis=0, concat_axis=1, tiled=True)


def solution(mesh):
    in_specs = (
        P(("seq", "row", "col"), None),
        P(("seq", "row", "col"), None),
        P(("seq", "row", "col"), None),
        P(("seq", "row", "col")),
        P(("row", "col"), None),
        P(("row", "col"), None),
        P(),
    )
    out_specs = P(("seq", "row", "col"), None)
    return jax.shard_map(
        on_device, mesh=mesh, in_specs=in_specs, out_specs=out_specs, check_vma=False
    )
```

profile of v0, /device:TPU:1, one launch (start us, length us, event | category | flops | bytes accessed | tf_op | source)
XLA Modules:
  0.0 255.7 jit_solution(11486921465186553433)
XLA Ops:
  6.5 1.0 copy-done
  7.6 0.6 constant_dynamic-slice_fusion.1
  8.3 10.5 %all-to-all-start.1 = ((bf16[4,32,256]{2,0,1:T(4,128)(2,1)}), bf16[4,32,256]{2,0,1:T(4,128)(2,1)S(1)}, u32[]{:S(2)}, u32[]{:S(2)}) async-start(bf16[4,32,256]{2,0,1:T(4,128)(2,1)} %bitcast.7), calls=%async_computation.1 | async-start | bytes 131072 | tf_op jit(solution)/shard_map/all_to_all | solution.py:66
  18.8 33.7 %all-gather = bf16[16,4,1024]{2,1,0:T(4,128)(2,1)S(1)} all-gather(bf16[1,4,1024]{2,1,0:T(4,128)(2,1)S(1)} %bitcast.165), channel_id=1, replica_groups=mesh['seq'=32,'row'=4,'col'=4] {'row','col'}, dimensions={0}, use_global_device_ids=true | all-gather | bytes 139264 | tf_op jit(solution)/shard_map/all_gather | solution.py:83
  52.6 0.9 broadcast_in_dim.118
  53.5 8.9 %all-to-all-start = ((bf16[64,32,128]{2,0,1:T(8,128)(2,1)}), bf16[64,32,128]{2,0,1:T(8,128)(2,1)S(1)}, u32[]{:S(2)}, u32[]{:S(2)}) async-start(bf16[64,32,128]{2,0,1:T(8,128)(2,1)} %bitcast.2), calls=%async_computation | async-start | bytes 1048576 | tf_op jit(solution)/shard_map/all_to_all | solution.py:87
  62.5 0.9 constant_dynamic-slice_fusion
  63.3 0.7 copy.73
  64.1 0.6 copy-done.16
  64.9 99.9 %all-reduce = s32[2048]{0:T(1024)S(1)} all-reduce(s32[2048]{0:T(1024)S(1)} %dynamic-update-slice), channel_id=1, replica_groups=mesh['seq'=32,'row'=4,'col'=4] {'seq','row','col'}, use_global_device_ids=true, to_apply=%add | all-reduce | flops 2048 | bytes 16384
  165.9 0.6 copy-done.13
  166.5 28.9 %all-gather.1 = bf16[16,4,1024]{2,1,0:T(4,128)(2,1)S(1)} all-gather(bf16[1,4,1024]{2,1,0:T(4,128)(2,1)S(1)} %bitcast.166), channel_id=1, replica_groups=mesh['seq'=32,'row'=4,'col'=4] {'row','col'}, dimensions={0}, use_global_device_ids=true | all-gather | bytes 139264 | tf_op jit(solution)/shard_map/all_gather | solution.py:84
  195.5 0.9 broadcast_in_dim.122
  196.4 7.4 %all-to-all-start.2 = ((bf16[64,32,128]{2,0,1:T(8,128)(2,1)}), bf16[64,32,128]{2,0,1:T(8,128)(2,1)S(1)}, u32[]{:S(2)}, u32[]{:S(2)}) async-start(bf16[64,32,128]{2,0,1:T(8,128)(2,1)} %bitcast.14), calls=%async_computation.2 | async-start | bytes 1048576 | tf_op jit(solution)/shard_map/all_to_all | solution.py:94
  203.8 2.1 broadcast_compare_fusion.5
  206.0 13.7 %all-to-all-done.2 = bf16[64,32,128]{2,0,1:T(8,128)(2,1)S(1)} async-done(((bf16[64,32,128]{2,0,1:T(8,128)(2,1)}), bf16[64,32,128]{2,0,1:T(8,128)(2,1)S(1)}, u32[]{:S(2)}, u32[]{:S(2)}) %all-to-all-start.2) | async-done | bytes 524320 | tf_op jit(solution)/shard_map/all_to_all | solution.py:94
  219.7 0.8 fusion.77
  221.3 1.4 select_reduce_fusion.1
  223.1 0.7 copy-done.9
  224.5 0.7 copy-done.11
  225.3 1.1 convolution_bitcast_fusion.4
  226.8 0.4 fusion.24
  227.2 0.4 fusion.28
  227.8 1.9 convolution_bitcast_fusion.3
  229.7 1.5 convolution_bitcast_fusion.2
  231.2 0.5 convolution_bitcast_fusion.1
  231.7 0.8 copy-done.4
  232.4 0.4 convolution_bitcast_fusion
  232.9 0.5 copy-done.10
  233.4 0.5 fusion.19
  234.1 14.1 %all_to_all.65 = bf16[32,4,256]{2,1,0:T(4,128)(2,1)S(1)} all-to-all(bf16[32,4,256]{2,1,0:T(4,128)(2,1)S(1)} %all_to_all.57), channel_id=1, replica_groups=mesh['seq'=32,'row'=4,'col'=4] {'seq'}, dimensions={0} | all-to-all | bytes 131072 | tf_op jit(solution)/shard_map/all_to_all | solution.py:120
  248.2 0.6 copy.101
  (62 shorter events, 3.4 us)
Async XLA Ops:
  6.5 1.0 copy-start
  6.5 214.7 %all-gather.5.cloned.1.call-start = ((), (), s32[]{:S(2)}) async-start(), calls=%async_computation.4 | async-start | bytes 1114112 | tf_op jit(solution)/shard_map/all_gather | solution.py:108
  8.2 10.5 %copy-start.12 = (bf16[4,1024]{1,0:T(4,128)(2,1)S(1)}, bf16[4,1024]{1,0:T(4,128)(2,1)}, u32[]{:S(2)}) copy-start(bf16[4,1024]{1,0:T(4,128)(2,1)} %param.8) | copy-start | bytes 24580
  8.3 44.3 %all-to-all-start.1 = ((bf16[4,32,256]{2,0,1:T(4,128)(2,1)}), bf16[4,32,256]{2,0,1:T(4,128)(2,1)S(1)}, u32[]{:S(2)}, u32[]{:S(2)}) async-start(bf16[4,32,256]{2,0,1:T(4,128)(2,1)} %bitcast.7), calls=%async_computation.1 | async-start | bytes 131072 | tf_op jit(solution)/shard_map/all_to_all | solution.py:66
  53.5 142.0 %all-to-all-start = ((bf16[64,32,128]{2,0,1:T(8,128)(2,1)}), bf16[64,32,128]{2,0,1:T(8,128)(2,1)S(1)}, u32[]{:S(2)}, u32[]{:S(2)}) async-start(bf16[64,32,128]{2,0,1:T(8,128)(2,1)} %bitcast.2), calls=%async_computation | async-start | bytes 1048576 | tf_op jit(solution)/shard_map/all_to_all | solution.py:87
  62.4 165.3 %all-gather.7.cloned.1.call-start = ((), (), s32[]{:S(2)}) async-start(), calls=%async_computation.5 | async-start | bytes 1114112 | tf_op jit(solution)/shard_map/all_gather | solution.py:109
  64.1 0.7 copy-start.16
  165.8 0.7 copy-start.13
  196.4 23.3 %all-to-all-start.2 = ((bf16[64,32,128]{2,0,1:T(8,128)(2,1)}), bf16[64,32,128]{2,0,1:T(8,128)(2,1)S(1)}, u32[]{:S(2)}, u32[]{:S(2)}) async-start(bf16[64,32,128]{2,0,1:T(8,128)(2,1)} %bitcast.14), calls=%async_computation.2 | async-start | bytes 1048576 | tf_op jit(solution)/shard_map/all_to_all | solution.py:94
  221.3 1.4 copy-start.15
  221.3 1.4 copy-start.8
  222.7 4.5 %copy-start.1 = (f32[128,1,2,1024]{0,3,2,1:T(8,128)}, f32[128,1,2,1024]{0,3,2,1:T(8,128)S(1)}, u32[]{:S(2)}) copy-start(f32[128,1,2,1024]{0,3,2,1:T(8,128)S(1)} %get-tuple-element.37) | copy-start | bytes 3145732
  222.7 1.1 copy-start.9
  223.1 3.7 %copy-start.5 = (f32[128,1,2,1024]{0,3,2,1:T(8,128)}, f32[128,1,2,1024]{0,3,2,1:T(8,128)S(1)}, u32[]{:S(2)}) copy-start(f32[128,1,2,1024]{0,3,2,1:T(8,128)S(1)} %get-tuple-element.39) | copy-start | bytes 3145732
  224.1 2.6 %copy-start.7 = (f32[128,1,2,1024]{0,3,2,1:T(8,128)}, f32[128,1,2,1024]{0,3,2,1:T(8,128)S(1)}, u32[]{:S(2)}) copy-start(f32[128,1,2,1024]{0,3,2,1:T(8,128)S(1)} %get-tuple-element.41) | copy-start | bytes 3145732
  224.1 1.1 copy-start.11
  224.5 2.7 %copy-start.3 = (f32[128,1,2,1024]{0,3,2,1:T(8,128)}, f32[128,1,2,1024]{0,3,2,1:T(8,128)S(1)}, u32[]{:S(2)}) copy-start(f32[128,1,2,1024]{0,3,2,1:T(8,128)S(1)} %get-tuple-element.35) | copy-start | bytes 3145732
  227.7 2.0 copy-start.6
  227.8 3.4 %copy-start.14 = (bf16[4096,128]{0,1:T(8,128)(2,1)S(1)}, bf16[4096,128]{0,1:T(8,128)(2,1)}, u32[]{:S(2)}) copy-start(bf16[4096,128]{0,1:T(8,128)(2,1)} %all-gather.7.cloned.1.call-done) | copy-start | bytes 3145732
  229.7 1.5 copy-start.2
  231.2 1.2 copy-start.4
  232.4 0.9 copy-start.10
  232.4 1.0 copy-start.17
Sparse Core Ops, SparseCore 0:
  9.4 71.4 all-gather.4
  82.9 63.6 all-gather.6
where the time goes:
time: 256 us
  blocking collectives  177 us (69%)
  starting transfers between devices  26.8 us (10%)
  between operations  14.5 us (6%)
  waiting for transfers between devices  13.8 us (5%)
  local copies, waits for them, and re-layouts  11.4 us (4%)
  matrix products  8.99 us (4%)
  other arithmetic  3.52 us (1%)
    unnamed x1, blocking collectives  99.9 us
    all_gather x1, blocking collectives, on_device(): lax.all_gather(new_keys, ('row', 'col'), axis=0, tiled=True)  33.7 us
    all_gather x1, blocking collectives, on_device(): lax.all_gather(new_values, ('row', 'col'), axis=0, tiled=True)  28.9 us
    all_to_all x1, blocking collectives, on_device(): lax.all_to_all(context, 'seq', split_axis=0, concat_axis=1, tiled=True)  14.1 us
    all_to_all x1, waiting for transfers between devices, on_device(): lax.all_to_all(spread_heads(grouped[1], seq_count, kv_dev, HD), 'seq', sp...  13.7 us
    all_to_all x1, starting transfers between devices, on_device(): lax.all_to_all(queries, 'seq', split_axis=1, concat_axis=0, tiled=True)  10.5 us
    all_to_all x1, starting transfers between devices, on_device(): lax.all_to_all(spread_heads(grouped[0], seq_count, kv_dev, HD), 'seq', sp...  8.93 us
    all_to_all x1, starting transfers between devices, on_device(): lax.all_to_all(spread_heads(grouped[1], seq_count, kv_dev, HD), 'seq', sp...  7.36 us
  transfers between devices with their start and end apart: 5, of which 1 were waited for; matrix products, arithmetic and copies ran while one was open for 5% of the time, Pallas kernels for 0%

commit v1 on v0

--- a/solution.py
+++ b/solution.py
@@ -80,7 +80,12 @@
         jnp.zeros((query_count, kv_dev, per_group, HD), jnp.float32),
     )
     grouped = (
-        lax.all_gather(new_keys, ("row", "col"), axis=0, tiled=True),
+        jnp.concatenate(
+            lax.all_to_all(
+                jnp.stack([new_keys] * lax.axis_size(("row", "col"))), ("row", "col"), 0, 0
+            ),
+            axis=0,
+        ),
         lax.all_gather(new_values, ("row", "col"), axis=0, tiled=True),
     )
     received = (

time: 256 us -> 240 us (0.938)
  blocking collectives: 177 us -> 165 us
  starting transfers between devices: 26.8 us -> 23.8 us
    all_gather x1 -> x0, blocking collectives: 33.7 us -> none  [on_device(): lax.all_gather(new_keys, ('row', 'col'), axis=0, tiled=True)]
    all_to_all x0 -> x1, blocking collectives: none -> 19.3 us  [on_device(): lax.all_to_all(queries, 'seq', split_axis=1, concat_axis=0, tiled=True)]
    all_to_all x1, waiting for transfers between devices: 13.7 us -> 0.01 us  [on_device(): lax.all_to_all(spread_heads(grouped[1], seq_count, kv_dev, HD), 'seq', sp...]
    all_to_all x1, waiting for transfers between devices: 0.01 us -> 12.2 us  [on_device(): lax.all_to_all(spread_heads(grouped[0], seq_count, kv_dev, HD), 'seq', sp...]
    all_to_all x1, starting transfers between devices: 7.36 us -> 3.89 us  [on_device(): lax.all_to_all(spread_heads(grouped[1], seq_count, kv_dev, HD), 'seq', sp...]
    unnamed x40 -> x38, local copies, waits for them, and re-layouts: 6.57 us -> 6.11 us
where the time goes in v1:
time: 240 us; the launch traced here: 239 us
  blocking collectives  165 us (69%)
  starting transfers between devices  23.8 us (10%)
  between operations  14.4 us (6%)
  waiting for transfers between devices  12.3 us (5%)
  local copies, waits for them, and re-layouts  11.7 us (5%)
  matrix products  8.98 us (4%)
  other arithmetic  2.59 us (1%)
    unnamed x1, blocking collectives  99.3 us
    all_gather x1, blocking collectives, on_device(): lax.all_gather(new_values, ('row', 'col'), axis=0, tiled=True)  30.1 us
    all_to_all x1, blocking collectives, on_device(): lax.all_to_all(queries, 'seq', split_axis=1, concat_axis=0, tiled=True)  19.3 us
    all_to_all x1, blocking collectives, on_device(): lax.all_to_all(context, 'seq', split_axis=0, concat_axis=1, tiled=True)  16.1 us
    all_to_all x1, starting transfers between devices, on_device(): lax.all_to_all(jnp.stack([new_keys] * lax.axis_size(('row', 'col'))), ('r...  12.6 us
    all_to_all x1, waiting for transfers between devices, on_device(): lax.all_to_all(spread_heads(grouped[0], seq_count, kv_dev, HD), 'seq', sp...  12.2 us
    all_to_all x1, starting transfers between devices, on_device(): lax.all_to_all(spread_heads(grouped[0], seq_count, kv_dev, HD), 'seq', sp...  7.3 us
    unnamed x38, local copies, waits for them, and re-layouts  6.11 us
  transfers between devices with their start and end apart: 5, of which 1 were waited for; matrix products, arithmetic and copies ran while one was open for 5% of the time, Pallas kernels for 0%

profile of v1, /device:TPU:1, one launch (start us, length us, event | category | flops | bytes accessed | tf_op | source)
XLA Modules:
  0.0 238.6 jit_solution(7832758550726782475)
XLA Ops:
  6.5 1.0 copy-done
  7.6 0.6 constant_dynamic-slice_fusion.1
  8.3 0.8 copy-done.10
  9.1 19.3 %all_to_all.70 = bf16[4,32,256]{2,0,1:T(4,128)(2,1)S(1)} all-to-all(bf16[4,32,256]{2,0,1:T(4,128)(2,1)S(1)} %bitcast.164), channel_id=1, replica_groups=mesh['seq'=32,'row'=4,'col'=4] {'seq'}, dimensions={1} | all-to-all | bytes 131072 | tf_op jit(solution)/shard_map/all_to_all | solution.py:66
  28.3 0.7 stack.2
  29.0 12.6 %all-to-all-start = ((bf16[16,4,1024]{2,1,0:T(4,128)(2,1)}), bf16[16,4,1024]{2,1,0:T(4,128)(2,1)S(1)}, u32[]{:S(2)}, u32[]{:S(2)}) async-start(bf16[16,4,1024]{2,1,0:T(4,128)(2,1)} %stack.2), calls=%async_computation | async-start | bytes 262144 | tf_op jit(solution)/shard_map/all_to_all | solution.py:84
  41.6 30.1 %all-gather = bf16[16,4,1024]{2,1,0:T(4,128)(2,1)S(1)} all-gather(bf16[1,4,1024]{2,1,0:T(4,128)(2,1)S(1)} %bitcast.165), channel_id=1, replica_groups=mesh['seq'=32,'row'=4,'col'=4] {'row','col'}, dimensions={0}, use_global_device_ids=true | all-gather | bytes 139264 | tf_op jit(solution)/shard_map/all_gather | solution.py:89
  71.8 0.9 broadcast_in_dim.122
  72.7 3.9 %all-to-all-start.3 = ((bf16[64,32,128]{2,0,1:T(8,128)(2,1)}), bf16[64,32,128]{2,0,1:T(8,128)(2,1)S(1)}, u32[]{:S(2)}, u32[]{:S(2)}) async-start(bf16[64,32,128]{2,0,1:T(8,128)(2,1)} %bitcast.13), calls=%async_computation.3 | async-start | bytes 1048576 | tf_op jit(solution)/shard_map/all_to_all | solution.py:99
  76.6 0.9 constant_dynamic-slice_fusion
  77.5 0.7 copy.72
  78.3 0.6 copy-done.15
  79.1 99.3 %all-reduce = s32[2048]{0:T(1024)S(1)} all-reduce(s32[2048]{0:T(1024)S(1)} %dynamic-update-slice), channel_id=1, replica_groups=mesh['seq'=32,'row'=4,'col'=4] {'seq','row','col'}, use_global_device_ids=true, to_apply=%add | all-reduce | flops 2048 | bytes 16384
  179.6 0.9 broadcast_in_dim.118
  180.5 7.3 %all-to-all-start.1 = ((bf16[64,32,128]{2,0,1:T(8,128)(2,1)}), bf16[64,32,128]{2,0,1:T(8,128)(2,1)S(1)}, u32[]{:S(2)}, u32[]{:S(2)}) async-start(bf16[64,32,128]{2,0,1:T(8,128)(2,1)} %bitcast.1), calls=%async_computation.1 | async-start | bytes 1048576 | tf_op jit(solution)/shard_map/all_to_all | solution.py:92
  187.9 1.2 broadcast_compare_fusion.5
  189.1 0.9 fusion.77
  190.0 12.2 %all-to-all-done.1 = bf16[64,32,128]{2,0,1:T(8,128)(2,1)S(1)} async-done(((bf16[64,32,128]{2,0,1:T(8,128)(2,1)}), bf16[64,32,128]{2,0,1:T(8,128)(2,1)S(1)}, u32[]{:S(2)}, u32[]{:S(2)}) %all-to-all-start.1) | async-done | bytes 524320 | tf_op jit(solution)/shard_map/all_to_all | solution.py:92
  202.9 1.4 select_reduce_fusion.1
  205.4 0.8 copy-done.9
  206.2 1.1 convolution_bitcast_fusion.4
  207.7 0.4 fusion.24
  208.2 0.4 fusion.28
  208.7 1.9 convolution_bitcast_fusion.3
  210.6 1.5 convolution_bitcast_fusion.2
  212.1 0.5 convolution_bitcast_fusion.1
  212.6 0.8 copy-done.4
  213.4 0.4 convolution_bitcast_fusion
  213.8 0.5 copy-done.8
  214.3 0.5 fusion.19
  215.0 16.1 %all_to_all.71 = bf16[32,4,256]{2,1,0:T(4,128)(2,1)S(1)} all-to-all(bf16[32,4,256]{2,1,0:T(4,128)(2,1)S(1)} %all_to_all.61), channel_id=1, replica_groups=mesh['seq'=32,'row'=4,'col'=4] {'seq'}, dimensions={0} | all-to-all | bytes 131072 | tf_op jit(solution)/shard_map/all_to_all | solution.py:125
  231.1 0.6 copy.100
  (61 shorter events, 3.4 us)
Async XLA Ops:
  6.5 1.0 copy-start
  6.5 196.4 %all-gather.4.cloned.1.call-start = ((), (), s32[]{:S(2)}) async-start(), calls=%async_computation.5 | async-start | bytes 1114112 | tf_op jit(solution)/shard_map/all_gather | solution.py:113
  8.2 0.8 copy-start.10
  9.1 19.3 %copy-start.11 = (bf16[4,1024]{1,0:T(4,128)(2,1)S(1)}, bf16[4,1024]{1,0:T(4,128)(2,1)}, u32[]{:S(2)}) copy-start(bf16[4,1024]{1,0:T(4,128)(2,1)} %param.8) | copy-start | bytes 24580
  29.0 12.6 %copy-start.12 = (bf16[4,1024]{1,0:T(4,128)(2,1)S(1)}, bf16[4,1024]{1,0:T(4,128)(2,1)}, u32[]{:S(2)}) copy-start(bf16[4,1024]{1,0:T(4,128)(2,1)} %param.9) | copy-start | bytes 24580
  29.0 42.7 %all-to-all-start = ((bf16[16,4,1024]{2,1,0:T(4,128)(2,1)}), bf16[16,4,1024]{2,1,0:T(4,128)(2,1)S(1)}, u32[]{:S(2)}, u32[]{:S(2)}) async-start(bf16[16,4,1024]{2,1,0:T(4,128)(2,1)} %stack.2), calls=%async_computation | async-start | bytes 262144 | tf_op jit(solution)/shard_map/all_to_all | solution.py:84
  72.7 106.9 %all-to-all-start.3 = ((bf16[64,32,128]{2,0,1:T(8,128)(2,1)}), bf16[64,32,128]{2,0,1:T(8,128)(2,1)S(1)}, u32[]{:S(2)}, u32[]{:S(2)}) async-start(bf16[64,32,128]{2,0,1:T(8,128)(2,1)} %bitcast.13), calls=%async_computation.3 | async-start | bytes 1048576 | tf_op jit(solution)/shard_map/all_to_all | solution.py:99
  76.6 132.1 %all-gather.6.cloned.1.call-start = ((), (), s32[]{:S(2)}) async-start(), calls=%async_computation.6 | async-start | bytes 1114112 | tf_op jit(solution)/shard_map/all_gather | solution.py:114
  78.2 0.7 copy-start.15
  180.5 21.6 %all-to-all-start.1 = ((bf16[64,32,128]{2,0,1:T(8,128)(2,1)}), bf16[64,32,128]{2,0,1:T(8,128)(2,1)S(1)}, u32[]{:S(2)}, u32[]{:S(2)}) async-start(bf16[64,32,128]{2,0,1:T(8,128)(2,1)} %bitcast.1), calls=%async_computation.1 | async-start | bytes 1048576 | tf_op jit(solution)/shard_map/all_to_all | solution.py:92
  202.9 1.4 copy-start.14
  204.3 3.8 %copy-start.1 = (f32[128,1,2,1024]{0,3,2,1:T(8,128)}, f32[128,1,2,1024]{0,3,2,1:T(8,128)S(1)}, u32[]{:S(2)}) copy-start(f32[128,1,2,1024]{0,3,2,1:T(8,128)S(1)} %get-tuple-element.37) | copy-start | bytes 3145732
  204.7 3.0 %copy-start.5 = (f32[128,1,2,1024]{0,3,2,1:T(8,128)}, f32[128,1,2,1024]{0,3,2,1:T(8,128)S(1)}, u32[]{:S(2)}) copy-start(f32[128,1,2,1024]{0,3,2,1:T(8,128)S(1)} %get-tuple-element.39) | copy-start | bytes 3145732
  205.0 2.7 %copy-start.7 = (f32[128,1,2,1024]{0,3,2,1:T(8,128)}, f32[128,1,2,1024]{0,3,2,1:T(8,128)S(1)}, u32[]{:S(2)}) copy-start(f32[128,1,2,1024]{0,3,2,1:T(8,128)S(1)} %get-tuple-element.41) | copy-start | bytes 3145732
  205.1 1.1 copy-start.9
  205.4 2.8 %copy-start.3 = (f32[128,1,2,1024]{0,3,2,1:T(8,128)}, f32[128,1,2,1024]{0,3,2,1:T(8,128)S(1)}, u32[]{:S(2)}) copy-start(f32[128,1,2,1024]{0,3,2,1:T(8,128)S(1)} %get-tuple-element.35) | copy-start | bytes 3145732
  208.6 2.0 copy-start.6
  208.7 3.4 %copy-start.13 = (bf16[4096,128]{0,1:T(8,128)(2,1)S(1)}, bf16[4096,128]{0,1:T(8,128)(2,1)}, u32[]{:S(2)}) copy-start(bf16[4096,128]{0,1:T(8,128)(2,1)} %all-gather.6.cloned.1.call-done) | copy-start | bytes 3145732
  210.6 1.5 copy-start.2
  212.1 1.2 copy-start.4
  213.4 0.9 copy-start.8
  213.4 1.0 copy-start.16
Sparse Core Ops, SparseCore 0:
  9.4 71.7 all-gather.3
  83.2 65.3 all-gather.5
